TPU v7x, 256 devices: a whole 4x4x8 slice. The times are simulated.
256 devices in a mesh: blk: 64 (over y, x_lo, z), team: 4 (over x_hi, core).
Axes of the slice: x: 4 (x_hi: 2, x_lo: 2; x = x_hi * 2 + x_lo), y: 4, z: 8, core: 2. Of those that a mesh axis runs over, the one named last changes fastest.
Arguments:
- loadings: bfloat16 [64, 98304], P(None, ('blk', 'team')), may hold values from -6 to 6
- scales: bfloat16 [64, 768], P(None, ('blk', 'team')), may hold values from 0.25 to 4
- cov: bfloat16 [16384, 16, 4, 1536], P('blk', None, 'team'), may hold values from -0.01953125 to 0.01953125
Outputs:
- product: float32 [64, 16384], P(None, 'blk')
All inputs are finite; a program needn't handle non-finite values.
Results may differ from a plain program's by a relative error of at most 0.0028.
Values may be sent and summed in bfloat16 or wider, within the bound.
No kernel may reach another device: no remote copies, remote signals or barrier semaphores. Data moves between devices by JAX's collectives and lax.ppermute only.
A program may use at most 128 MiB of HBM per device.

v0:
```python
import jax
import jax.numpy as jnp
from jax import lax
from jax.sharding import PartitionSpec as P


def passed_along(x, axis, by):
    size = lax.axis_size(axis)
    return lax.ppermute(x, axis, [(i, (i + by) % size) for i in range(size)])


def per_device(loadings, scales, cov):
    team_size = lax.axis_size("team")
    cycle_size = lax.axis_size("blk")
    cycle_stops = cycle_size // team_size
    cycle_pos = lax.axis_index("blk")
    member = lax.axis_index("team")
    skew_lag = jnp.mod(cycle_pos - member, team_size)
    base_stop = jnp.mod((cycle_pos - skew_lag - member) // team_size, cycle_stops)
    held_block = (
        lax.all_gather(loadings, "team", axis=1, tiled=True),
        lax.all_gather(scales, "team", axis=1, tiled=True),
    )
    near_copy = passed_along((held_block[0], held_block[1]), "blk", 1)
    far_copies = passed_along((held_block[0], held_block[1], near_copy[0], near_copy[1]), "blk", 2)
    stacked_loads = jnp.stack([held_block[0], near_copy[0], far_copies[0], far_copies[2]])
    stacked_scales = jnp.stack([held_block[1], near_copy[1], far_copies[1], far_copies[3]])
    start_block = (
        lax.dynamic_index_in_dim(stacked_loads, skew_lag, 0, keepdims=False),
        lax.dynamic_index_in_dim(stacked_scales, skew_lag, 0, keepdims=False),
    )
    cov_local = cov[:, :, 0, :]
    n_loads = loadings.shape[0]
    row_count = cov.shape[0]

    def contribute(running, block, stop_num):
        block_load, block_scale = block
        groups = block_scale.shape[1]
        scaled = (
            (
                block_load.astype(jnp.float32).reshape(
                    n_loads, groups, block_load.shape[1] // groups
                )
                * block_scale.astype(jnp.float32)[:, :, None]
            )
            .reshape(n_loads, block_load.shape[1])
            .astype(jnp.bfloat16)
        )
        cov_slab = lax.dynamic_index_in_dim(
            cov_local, jnp.mod(stop_num, cycle_stops), 1, keepdims=False
        )
        term = lax.dot_general(
            scaled, cov_slab, (((1,), (1,)), ((), ())), preferred_element_type=jnp.float32
        )
        return running + term

    initial = jnp.zeros((n_loads, row_count), jnp.float32)
    running = contribute(initial, start_block, base_stop)

    def onward(stop_num, carry):
        partial_sum, moving = carry
        moving = passed_along((moving[0], moving[1]), "blk", team_size)
        return (contribute(partial_sum, moving, base_stop - stop_num), moving)

    running, _ = lax.fori_loop(1, cycle_stops, onward, (running, start_block))
    product = lax.psum(running, "team")
    return product


def solution(mesh):
    placed = (P(None, ("blk", "team")), P(None, ("blk", "team")), P("blk", None, "team", None))
    return jax.shard_map(
        per_device, mesh=mesh, in_specs=placed, out_specs=P(None, "blk"), check_vma=False
    )
```

profile of v0, /device:TPU:1, one launch (start us, length us, event | category | flops | bytes accessed | tf_op | source)
XLA Modules:
  0.0 371.3 jit_solution(5446585981449639470)
XLA Ops:
  6.5 10.4 %all_gather.6 = bf16[64,1536]{1,0:T(8,128)(2,1)S(1)} all-gather(bf16[64,384]{1,0:T(8,128)(2,1)} %param.5), channel_id=1, replica_groups=mesh['blk'=64,'team'=4] {'team'}, dimensions={1}, use_global_device_ids=true | all-gather | bytes 245760 | tf_op jit(solution)/shard_map/all_gather | solution.py:21
  16.9 2.9 collective-permute-start.3
  19.8 7.4 %all-gather = bf16[4,3,64]{2,1,0:T(4,128)(2,1)S(1)} all-gather(bf16[1,3,64]{2,1,0:T(4,128)(2,1)} %bitcast.55), channel_id=1, replica_groups=mesh['blk'=64,'team'=4] {'team'}, dimensions={0}, use_global_device_ids=true | all-gather | bytes 1920 | tf_op jit(solution)/shard_map/all_gather | solution.py:22
  27.2 2.9 collective-permute-start.5
  31.2 6.3 %collective-permute-done.5 = bf16[64,12]{0,1:T(8,128)(2,1)S(1)} collective-permute-done((bf16[64,12]{0,1:T(8,128)(2,1)S(1)}, bf16[64,12]{0,1:T(8,128)(2,1)S(1)}, u32[]{:S(2)}, u32[]{:S(2)}) %collective-permute-start.5) | collective-permute-done | bytes 1568 | tf_op jit(solution)/shard_map/ppermute | solution.py:9
  38.2 4.4 %constant_dynamic-slice_fusion = bf16[256,1,1,1536]{3,1,2,0:T(2,128)(2,1)S(1)} fusion(bf16[256,16,1,1536]{3,1,2,0:T(8,128)(2,1)} %param.7, s32[]{:T(128)S(6)} %select_n.61), kind=kLoop, calls=%fused_computation.27 | loop fusion | bytes 1572868 | tf_op jit(solution)/shard_map/jit(dynamic_index_in_dim)/dynamic_slice | solution.py:49
  42.7 13.0 %copy.27 = bf16[256,16,1,1536]{3,0,1,2:T(8,128)(2,1)} copy(bf16[256,16,1,1536]{3,1,2,0:T(8,128)(2,1)} %param.7) | data formatting | bytes 25165824 | tf_op args[2]
  56.8 219.6 %while.19 = (s32[]{:T(128)}, f32[64,256]{1,0:T(8,128)S(1)}, bf16[64,1536]{1,0:T(8,128)(2,1)S(1)}, bf16[64,12]{1,0:T(8,128)(2,1)S(1)}, s32[]{:T(128)}, /*index=5*...) while((s32[]{:T(128)}, f32[64,256]{1,0:T(8,128)S(1)}, ...), condition=%wide.region_1.2_spmd, body=%wide.region_0.1_spmd.sunk | while | flops 50642960 | bytes 3091284 | solution.py:65
  56.9 2.6 collective-permute-start.1
  59.4 3.8 %collective-permute-start = (bf16[64,12]{1,0:T(8,128)(2,1)S(1)}, bf16[64,12]{1,0:T(8,128)(2,1)S(1)}, u32[]{:S(2)}, u32[]{:S(2)}) collective-permute-start(bf16[64,12]{1,0:T(8,128)(2,1)S(1)} %get-tuple-element.235), channel_id=1, source_target_pairs={{0,16},{4,20},{8,24},{12,28},{16,32},{20,36},{24,40},{28,44},{32,4... | collective-permute-start | bytes 4616 | tf_op jit(solution)/shard_map/while/body/eval_jaxpr/ppermute | solution.py:9
  63.2 8.5 %collective-permute-done = bf16[64,12]{1,0:T(8,128)(2,1)S(1)} collective-permute-done((bf16[64,12]{1,0:T(8,128)(2,1)S(1)}, bf16[64,12]{1,0:T(8,128)(2,1)S(1)}, u32[]{:S(2)}, u32[]{:S(2)}) %collective-permute-start) | collective-permute-done | bytes 1568 | tf_op jit(solution)/shard_map/while/body/eval_jaxpr/ppermute | solution.py:9
  74.2 5.7 %collective-permute-start = (bf16[64,12]{1,0:T(8,128)(2,1)S(1)}, bf16[64,12]{1,0:T(8,128)(2,1)S(1)}, u32[]{:S(2)}, u32[]{:S(2)}) collective-permute-start(bf16[64,12]{1,0:T(8,128)(2,1)S(1)} %get-tuple-element.235), channel_id=1, source_target_pairs={{0,16},{4,20},{8,24},{12,28},{16,32},{20,36},{24,40},{28,44},{32,4... | collective-permute-start | bytes 4616 | tf_op jit(solution)/shard_map/while/body/eval_jaxpr/ppermute | solution.py:9
  79.9 11.1 %collective-permute-done = bf16[64,12]{1,0:T(8,128)(2,1)S(1)} collective-permute-done((bf16[64,12]{1,0:T(8,128)(2,1)S(1)}, bf16[64,12]{1,0:T(8,128)(2,1)S(1)}, u32[]{:S(2)}, u32[]{:S(2)}) %collective-permute-start) | collective-permute-done | bytes 1568 | tf_op jit(solution)/shard_map/while/body/eval_jaxpr/ppermute | solution.py:9
  94.8 10.4 %collective-permute-done = bf16[64,12]{1,0:T(8,128)(2,1)S(1)} collective-permute-done((bf16[64,12]{1,0:T(8,128)(2,1)S(1)}, bf16[64,12]{1,0:T(8,128)(2,1)S(1)}, u32[]{:S(2)}, u32[]{:S(2)}) %collective-permute-start) | collective-permute-done | bytes 1568 | tf_op jit(solution)/shard_map/while/body/eval_jaxpr/ppermute | solution.py:9
  107.0 3.6 collective-permute-start
  110.6 8.2 %collective-permute-done = bf16[64,12]{1,0:T(8,128)(2,1)S(1)} collective-permute-done((bf16[64,12]{1,0:T(8,128)(2,1)S(1)}, bf16[64,12]{1,0:T(8,128)(2,1)S(1)}, u32[]{:S(2)}, u32[]{:S(2)}) %collective-permute-start) | collective-permute-done | bytes 1568 | tf_op jit(solution)/shard_map/while/body/eval_jaxpr/ppermute | solution.py:9
  120.6 4.6 %collective-permute-start = (bf16[64,12]{1,0:T(8,128)(2,1)S(1)}, bf16[64,12]{1,0:T(8,128)(2,1)S(1)}, u32[]{:S(2)}, u32[]{:S(2)}) collective-permute-start(bf16[64,12]{1,0:T(8,128)(2,1)S(1)} %get-tuple-element.235), channel_id=1, source_target_pairs={{0,16},{4,20},{8,24},{12,28},{16,32},{20,36},{24,40},{28,44},{32,4... | collective-permute-start | bytes 4616 | tf_op jit(solution)/shard_map/while/body/eval_jaxpr/ppermute | solution.py:9
  125.2 7.1 %collective-permute-done = bf16[64,12]{1,0:T(8,128)(2,1)S(1)} collective-permute-done((bf16[64,12]{1,0:T(8,128)(2,1)S(1)}, bf16[64,12]{1,0:T(8,128)(2,1)S(1)}, u32[]{:S(2)}, u32[]{:S(2)}) %collective-permute-start) | collective-permute-done | bytes 1568 | tf_op jit(solution)/shard_map/while/body/eval_jaxpr/ppermute | solution.py:9
  134.1 5.4 %collective-permute-start = (bf16[64,12]{1,0:T(8,128)(2,1)S(1)}, bf16[64,12]{1,0:T(8,128)(2,1)S(1)}, u32[]{:S(2)}, u32[]{:S(2)}) collective-permute-start(bf16[64,12]{1,0:T(8,128)(2,1)S(1)} %get-tuple-element.235), channel_id=1, source_target_pairs={{0,16},{4,20},{8,24},{12,28},{16,32},{20,36},{24,40},{28,44},{32,4... | collective-permute-start | bytes 4616 | tf_op jit(solution)/shard_map/while/body/eval_jaxpr/ppermute | solution.py:9
  139.5 6.3 %collective-permute-done = bf16[64,12]{1,0:T(8,128)(2,1)S(1)} collective-permute-done((bf16[64,12]{1,0:T(8,128)(2,1)S(1)}, bf16[64,12]{1,0:T(8,128)(2,1)S(1)}, u32[]{:S(2)}, u32[]{:S(2)}) %collective-permute-start) | collective-permute-done | bytes 1568 | tf_op jit(solution)/shard_map/while/body/eval_jaxpr/ppermute | solution.py:9
  147.8 6.4 %collective-permute-start = (bf16[64,12]{1,0:T(8,128)(2,1)S(1)}, bf16[64,12]{1,0:T(8,128)(2,1)S(1)}, u32[]{:S(2)}, u32[]{:S(2)}) collective-permute-start(bf16[64,12]{1,0:T(8,128)(2,1)S(1)} %get-tuple-element.235), channel_id=1, source_target_pairs={{0,16},{4,20},{8,24},{12,28},{16,32},{20,36},{24,40},{28,44},{32,4... | collective-permute-start | bytes 4616 | tf_op jit(solution)/shard_map/while/body/eval_jaxpr/ppermute | solution.py:9
  154.2 5.0 %collective-permute-done = bf16[64,12]{1,0:T(8,128)(2,1)S(1)} collective-permute-done((bf16[64,12]{1,0:T(8,128)(2,1)S(1)}, bf16[64,12]{1,0:T(8,128)(2,1)S(1)}, u32[]{:S(2)}, u32[]{:S(2)}) %collective-permute-start) | collective-permute-done | bytes 1568 | tf_op jit(solution)/shard_map/while/body/eval_jaxpr/ppermute | solution.py:9
  162.6 3.0 collective-permute-start
  165.6 7.0 %collective-permute-done = bf16[64,12]{1,0:T(8,128)(2,1)S(1)} collective-permute-done((bf16[64,12]{1,0:T(8,128)(2,1)S(1)}, bf16[64,12]{1,0:T(8,128)(2,1)S(1)}, u32[]{:S(2)}, u32[]{:S(2)}) %collective-permute-start) | collective-permute-done | bytes 1568 | tf_op jit(solution)/shard_map/while/body/eval_jaxpr/ppermute | solution.py:9
  177.0 10.0 %collective-permute-done = bf16[64,12]{1,0:T(8,128)(2,1)S(1)} collective-permute-done((bf16[64,12]{1,0:T(8,128)(2,1)S(1)}, bf16[64,12]{1,0:T(8,128)(2,1)S(1)}, u32[]{:S(2)}, u32[]{:S(2)}) %collective-permute-start) | collective-permute-done | bytes 1568 | tf_op jit(solution)/shard_map/while/body/eval_jaxpr/ppermute | solution.py:9
  190.2 12.2 %collective-permute-done = bf16[64,12]{1,0:T(8,128)(2,1)S(1)} collective-permute-done((bf16[64,12]{1,0:T(8,128)(2,1)S(1)}, bf16[64,12]{1,0:T(8,128)(2,1)S(1)}, u32[]{:S(2)}, u32[]{:S(2)}) %collective-permute-start) | collective-permute-done | bytes 1568 | tf_op jit(solution)/shard_map/while/body/eval_jaxpr/ppermute | solution.py:9
  204.3 13.2 %collective-permute-done = bf16[64,12]{1,0:T(8,128)(2,1)S(1)} collective-permute-done((bf16[64,12]{1,0:T(8,128)(2,1)S(1)}, bf16[64,12]{1,0:T(8,128)(2,1)S(1)}, u32[]{:S(2)}, u32[]{:S(2)}) %collective-permute-start) | collective-permute-done | bytes 1568 | tf_op jit(solution)/shard_map/while/body/eval_jaxpr/ppermute | solution.py:9
  219.4 14.1 %collective-permute-done = bf16[64,12]{1,0:T(8,128)(2,1)S(1)} collective-permute-done((bf16[64,12]{1,0:T(8,128)(2,1)S(1)}, bf16[64,12]{1,0:T(8,128)(2,1)S(1)}, u32[]{:S(2)}, u32[]{:S(2)}) %collective-permute-start) | collective-permute-done | bytes 1568 | tf_op jit(solution)/shard_map/while/body/eval_jaxpr/ppermute | solution.py:9
  235.5 12.3 %collective-permute-done = bf16[64,12]{1,0:T(8,128)(2,1)S(1)} collective-permute-done((bf16[64,12]{1,0:T(8,128)(2,1)S(1)}, bf16[64,12]{1,0:T(8,128)(2,1)S(1)}, u32[]{:S(2)}, u32[]{:S(2)}) %collective-permute-start) | collective-permute-done | bytes 1568 | tf_op jit(solution)/shard_map/while/body/eval_jaxpr/ppermute | solution.py:9
  250.1 11.1 %collective-permute-done = bf16[64,12]{1,0:T(8,128)(2,1)S(1)} collective-permute-done((bf16[64,12]{1,0:T(8,128)(2,1)S(1)}, bf16[64,12]{1,0:T(8,128)(2,1)S(1)}, u32[]{:S(2)}, u32[]{:S(2)}) %collective-permute-start) | collective-permute-done | bytes 1568 | tf_op jit(solution)/shard_map/while/body/eval_jaxpr/ppermute | solution.py:9
  264.2 10.6 %collective-permute-done = bf16[64,12]{1,0:T(8,128)(2,1)S(1)} collective-permute-done((bf16[64,12]{1,0:T(8,128)(2,1)S(1)}, bf16[64,12]{1,0:T(8,128)(2,1)S(1)}, u32[]{:S(2)}, u32[]{:S(2)}) %collective-permute-start) | collective-permute-done | bytes 1568 | tf_op jit(solution)/shard_map/while/body/eval_jaxpr/ppermute | solution.py:9
  277.1 85.8 %all-reduce.2.cloned.1.call-done = f32[64,256]{1,0:T(8,128)} async-done(((f32[64,256]{1,0:T(8,128)}), f32[64,256]{1,0:T(8,128)}) %all-reduce.2.cloned.1.call-update) | async-done | bytes 65552 | tf_op jit(solution)/shard_map/psum | solution.py:66
  (119 shorter events, 42.0 us)
Async XLA Ops:
  6.5 356.4 %all-reduce.2.cloned.1.call-start = ((), (), s32[]{:S(2)}) async-start(), calls=%async_computation | async-start | bytes 131072 | tf_op jit(solution)/shard_map/psum | solution.py:66
  16.9 20.6 %collective-permute-start.2 = (bf16[64,1536]{1,0:T(8,128)(2,1)S(1)}, bf16[64,1536]{1,0:T(8,128)(2,1)S(1)}, u32[]{:S(2)}, u32[]{:S(2)}) collective-permute-start(bf16[64,1536]{1,0:T(8,128)(2,1)S(1)} %all_gather.6), channel_id=1, source_target_pairs={{0,4},{4,8},{8,12},{12,16},{16,20},{20,24},{24,28},{28,32},{32,36}... | collective-permute-start | bytes 589832 | tf_op jit(solution)/shard_map/ppermute | solution.py:9
  16.9 39.0 %collective-permute-start.3 = (bf16[64,1536]{1,0:T(8,128)(2,1)S(1)}, bf16[64,1536]{1,0:T(8,128)(2,1)S(1)}, u32[]{:S(2)}, u32[]{:S(2)}) collective-permute-start(bf16[64,1536]{1,0:T(8,128)(2,1)S(1)} %all_gather.6), channel_id=1, source_target_pairs={{0,8},{4,12},{8,16},{12,20},{16,24},{20,28},{24,32},{28,36},{32,40... | collective-permute-start | bytes 589832 | tf_op jit(solution)/shard_map/ppermute | solution.py:9
  30.0 25.6 %collective-permute-start.6 = (bf16[64,12]{0,1:T(8,128)(2,1)S(1)}, bf16[64,12]{0,1:T(8,128)(2,1)S(1)}, u32[]{:S(2)}, u32[]{:S(2)}) collective-permute-start(bf16[64,12]{0,1:T(8,128)(2,1)S(1)} %bitcast.50), channel_id=1, source_target_pairs={{0,8},{4,12},{8,16},{12,20},{16,24},{20,28},{24,32},{28,36},{32,40... | collective-permute-start | bytes 4616 | tf_op jit(solution)/shard_map/ppermute | solution.py:9
  37.6 18.1 %collective-permute-start.7 = (bf16[64,12]{0,1:T(8,128)(2,1)S(1)}, bf16[64,12]{0,1:T(8,128)(2,1)S(1)}, u32[]{:S(2)}, u32[]{:S(2)}) collective-permute-start(bf16[64,12]{0,1:T(8,128)(2,1)S(1)} %collective-permute-done.5), channel_id=1, source_target_pairs={{0,8},{4,12},{8,16},{12,20},{16,24},{20,28},{24,32},{28,36},{32,40... | collective-permute-start | bytes 4616 | tf_op jit(solution)/shard_map/ppermute | solution.py:9
  37.6 18.4 %collective-permute-start.4 = (bf16[64,1536]{1,0:T(8,128)(2,1)S(1)}, bf16[64,1536]{1,0:T(8,128)(2,1)S(1)}, u32[]{:S(2)}, u32[]{:S(2)}) collective-permute-start(bf16[64,1536]{1,0:T(8,128)(2,1)S(1)} %collective-permute-done.2), channel_id=1, source_target_pairs={{0,8},{4,12},{8,16},{12,20},{16,24},{20,28},{24,32},{28,36},{32,40... | collective-permute-start | bytes 589832 | tf_op jit(solution)/shard_map/ppermute | solution.py:9
  56.9 14.9 %collective-permute-start.1 = (bf16[64,1536]{1,0:T(8,128)(2,1)S(1)}, bf16[64,1536]{1,0:T(8,128)(2,1)S(1)}, u32[]{:S(2)}, u32[]{:S(2)}) collective-permute-start(bf16[64,1536]{1,0:T(8,128)(2,1)S(1)} %get-tuple-element.234), channel_id=1, source_target_pairs={{0,16},{4,20},{8,24},{12,28},{16,32},{20,36},{24,40},{28,44},{32,4... | collective-permute-start | bytes 589832 | tf_op jit(solution)/shard_map/while/body/eval_jaxpr/ppermute | solution.py:9
  59.4 12.3 %collective-permute-start = (bf16[64,12]{1,0:T(8,128)(2,1)S(1)}, bf16[64,12]{1,0:T(8,128)(2,1)S(1)}, u32[]{:S(2)}, u32[]{:S(2)}) collective-permute-start(bf16[64,12]{1,0:T(8,128)(2,1)S(1)} %get-tuple-element.235), channel_id=1, source_target_pairs={{0,16},{4,20},{8,24},{12,28},{16,32},{20,36},{24,40},{28,44},{32,4... | collective-permute-start | bytes 4616 | tf_op jit(solution)/shard_map/while/body/eval_jaxpr/ppermute | solution.py:9
  73.4 17.6 %collective-permute-start.1 = (bf16[64,1536]{1,0:T(8,128)(2,1)S(1)}, bf16[64,1536]{1,0:T(8,128)(2,1)S(1)}, u32[]{:S(2)}, u32[]{:S(2)}) collective-permute-start(bf16[64,1536]{1,0:T(8,128)(2,1)S(1)} %get-tuple-element.234), channel_id=1, source_target_pairs={{0,16},{4,20},{8,24},{12,28},{16,32},{20,36},{24,40},{28,44},{32,4... | collective-permute-start | bytes 589832 | tf_op jit(solution)/shard_map/while/body/eval_jaxpr/ppermute | solution.py:9
  74.2 16.8 %collective-permute-start = (bf16[64,12]{1,0:T(8,128)(2,1)S(1)}, bf16[64,12]{1,0:T(8,128)(2,1)S(1)}, u32[]{:S(2)}, u32[]{:S(2)}) collective-permute-start(bf16[64,12]{1,0:T(8,128)(2,1)S(1)} %get-tuple-element.235), channel_id=1, source_target_pairs={{0,16},{4,20},{8,24},{12,28},{16,32},{20,36},{24,40},{28,44},{32,4... | collective-permute-start | bytes 4616 | tf_op jit(solution)/shard_map/while/body/eval_jaxpr/ppermute | solution.py:9
  92.7 12.5 %collective-permute-start.1 = (bf16[64,1536]{1,0:T(8,128)(2,1)S(1)}, bf16[64,1536]{1,0:T(8,128)(2,1)S(1)}, u32[]{:S(2)}, u32[]{:S(2)}) collective-permute-start(bf16[64,1536]{1,0:T(8,128)(2,1)S(1)} %get-tuple-element.234), channel_id=1, source_target_pairs={{0,16},{4,20},{8,24},{12,28},{16,32},{20,36},{24,40},{28,44},{32,4... | collective-permute-start | bytes 589832 | tf_op jit(solution)/shard_map/while/body/eval_jaxpr/ppermute | solution.py:9
  92.8 12.4 %collective-permute-start = (bf16[64,12]{1,0:T(8,128)(2,1)S(1)}, bf16[64,12]{1,0:T(8,128)(2,1)S(1)}, u32[]{:S(2)}, u32[]{:S(2)}) collective-permute-start(bf16[64,12]{1,0:T(8,128)(2,1)S(1)} %get-tuple-element.235), channel_id=1, source_target_pairs={{0,16},{4,20},{8,24},{12,28},{16,32},{20,36},{24,40},{28,44},{32,4... | collective-permute-start | bytes 4616 | tf_op jit(solution)/shard_map/while/body/eval_jaxpr/ppermute | solution.py:9
  106.9 11.9 %collective-permute-start.1 = (bf16[64,1536]{1,0:T(8,128)(2,1)S(1)}, bf16[64,1536]{1,0:T(8,128)(2,1)S(1)}, u32[]{:S(2)}, u32[]{:S(2)}) collective-permute-start(bf16[64,1536]{1,0:T(8,128)(2,1)S(1)} %get-tuple-element.234), channel_id=1, source_target_pairs={{0,16},{4,20},{8,24},{12,28},{16,32},{20,36},{24,40},{28,44},{32,4... | collective-permute-start | bytes 589832 | tf_op jit(solution)/shard_map/while/body/eval_jaxpr/ppermute | solution.py:9
  107.0 11.8 %collective-permute-start = (bf16[64,12]{1,0:T(8,128)(2,1)S(1)}, bf16[64,12]{1,0:T(8,128)(2,1)S(1)}, u32[]{:S(2)}, u32[]{:S(2)}) collective-permute-start(bf16[64,12]{1,0:T(8,128)(2,1)S(1)} %get-tuple-element.235), channel_id=1, source_target_pairs={{0,16},{4,20},{8,24},{12,28},{16,32},{20,36},{24,40},{28,44},{32,4... | collective-permute-start | bytes 4616 | tf_op jit(solution)/shard_map/while/body/eval_jaxpr/ppermute | solution.py:9
  120.5 11.8 %collective-permute-start.1 = (bf16[64,1536]{1,0:T(8,128)(2,1)S(1)}, bf16[64,1536]{1,0:T(8,128)(2,1)S(1)}, u32[]{:S(2)}, u32[]{:S(2)}) collective-permute-start(bf16[64,1536]{1,0:T(8,128)(2,1)S(1)} %get-tuple-element.234), channel_id=1, source_target_pairs={{0,16},{4,20},{8,24},{12,28},{16,32},{20,36},{24,40},{28,44},{32,4... | collective-permute-start | bytes 589832 | tf_op jit(solution)/shard_map/while/body/eval_jaxpr/ppermute | solution.py:9
  120.6 11.7 %collective-permute-start = (bf16[64,12]{1,0:T(8,128)(2,1)S(1)}, bf16[64,12]{1,0:T(8,128)(2,1)S(1)}, u32[]{:S(2)}, u32[]{:S(2)}) collective-permute-start(bf16[64,12]{1,0:T(8,128)(2,1)S(1)} %get-tuple-element.235), channel_id=1, source_target_pairs={{0,16},{4,20},{8,24},{12,28},{16,32},{20,36},{24,40},{28,44},{32,4... | collective-permute-start | bytes 4616 | tf_op jit(solution)/shard_map/while/body/eval_jaxpr/ppermute | solution.py:9
  134.0 11.7 %collective-permute-start.1 = (bf16[64,1536]{1,0:T(8,128)(2,1)S(1)}, bf16[64,1536]{1,0:T(8,128)(2,1)S(1)}, u32[]{:S(2)}, u32[]{:S(2)}) collective-permute-start(bf16[64,1536]{1,0:T(8,128)(2,1)S(1)} %get-tuple-element.234), channel_id=1, source_target_pairs={{0,16},{4,20},{8,24},{12,28},{16,32},{20,36},{24,40},{28,44},{32,4... | collective-permute-start | bytes 589832 | tf_op jit(solution)/shard_map/while/body/eval_jaxpr/ppermute | solution.py:9
  147.5 11.7 %collective-permute-start.1 = (bf16[64,1536]{1,0:T(8,128)(2,1)S(1)}, bf16[64,1536]{1,0:T(8,128)(2,1)S(1)}, u32[]{:S(2)}, u32[]{:S(2)}) collective-permute-start(bf16[64,1536]{1,0:T(8,128)(2,1)S(1)} %get-tuple-element.234), channel_id=1, source_target_pairs={{0,16},{4,20},{8,24},{12,28},{16,32},{20,36},{24,40},{28,44},{32,4... | collective-permute-start | bytes 589832 | tf_op jit(solution)/shard_map/while/body/eval_jaxpr/ppermute | solution.py:9
  160.9 11.7 %collective-permute-start.1 = (bf16[64,1536]{1,0:T(8,128)(2,1)S(1)}, bf16[64,1536]{1,0:T(8,128)(2,1)S(1)}, u32[]{:S(2)}, u32[]{:S(2)}) collective-permute-start(bf16[64,1536]{1,0:T(8,128)(2,1)S(1)} %get-tuple-element.234), channel_id=1, source_target_pairs={{0,16},{4,20},{8,24},{12,28},{16,32},{20,36},{24,40},{28,44},{32,4... | collective-permute-start | bytes 589832 | tf_op jit(solution)/shard_map/while/body/eval_jaxpr/ppermute | solution.py:9
  174.3 12.6 %collective-permute-start.1 = (bf16[64,1536]{1,0:T(8,128)(2,1)S(1)}, bf16[64,1536]{1,0:T(8,128)(2,1)S(1)}, u32[]{:S(2)}, u32[]{:S(2)}) collective-permute-start(bf16[64,1536]{1,0:T(8,128)(2,1)S(1)} %get-tuple-element.234), channel_id=1, source_target_pairs={{0,16},{4,20},{8,24},{12,28},{16,32},{20,36},{24,40},{28,44},{32,4... | collective-permute-start | bytes 589832 | tf_op jit(solution)/shard_map/while/body/eval_jaxpr/ppermute | solution.py:9
  175.1 11.8 %collective-permute-start = (bf16[64,12]{1,0:T(8,128)(2,1)S(1)}, bf16[64,12]{1,0:T(8,128)(2,1)S(1)}, u32[]{:S(2)}, u32[]{:S(2)}) collective-permute-start(bf16[64,12]{1,0:T(8,128)(2,1)S(1)} %get-tuple-element.235), channel_id=1, source_target_pairs={{0,16},{4,20},{8,24},{12,28},{16,32},{20,36},{24,40},{28,44},{32,4... | collective-permute-start | bytes 4616 | tf_op jit(solution)/shard_map/while/body/eval_jaxpr/ppermute | solution.py:9
  188.6 13.7 %collective-permute-start.1 = (bf16[64,1536]{1,0:T(8,128)(2,1)S(1)}, bf16[64,1536]{1,0:T(8,128)(2,1)S(1)}, u32[]{:S(2)}, u32[]{:S(2)}) collective-permute-start(bf16[64,1536]{1,0:T(8,128)(2,1)S(1)} %get-tuple-element.234), channel_id=1, source_target_pairs={{0,16},{4,20},{8,24},{12,28},{16,32},{20,36},{24,40},{28,44},{32,4... | collective-permute-start | bytes 589832 | tf_op jit(solution)/shard_map/while/body/eval_jaxpr/ppermute | solution.py:9
  188.7 13.6 %collective-permute-start = (bf16[64,12]{1,0:T(8,128)(2,1)S(1)}, bf16[64,12]{1,0:T(8,128)(2,1)S(1)}, u32[]{:S(2)}, u32[]{:S(2)}) collective-permute-start(bf16[64,12]{1,0:T(8,128)(2,1)S(1)} %get-tuple-element.235), channel_id=1, source_target_pairs={{0,16},{4,20},{8,24},{12,28},{16,32},{20,36},{24,40},{28,44},{32,4... | collective-permute-start | bytes 4616 | tf_op jit(solution)/shard_map/while/body/eval_jaxpr/ppermute | solution.py:9
  204.1 13.4 %collective-permute-start.1 = (bf16[64,1536]{1,0:T(8,128)(2,1)S(1)}, bf16[64,1536]{1,0:T(8,128)(2,1)S(1)}, u32[]{:S(2)}, u32[]{:S(2)}) collective-permute-start(bf16[64,1536]{1,0:T(8,128)(2,1)S(1)} %get-tuple-element.234), channel_id=1, source_target_pairs={{0,16},{4,20},{8,24},{12,28},{16,32},{20,36},{24,40},{28,44},{32,4... | collective-permute-start | bytes 589832 | tf_op jit(solution)/shard_map/while/body/eval_jaxpr/ppermute | solution.py:9
  204.1 13.3 %collective-permute-start = (bf16[64,12]{1,0:T(8,128)(2,1)S(1)}, bf16[64,12]{1,0:T(8,128)(2,1)S(1)}, u32[]{:S(2)}, u32[]{:S(2)}) collective-permute-start(bf16[64,12]{1,0:T(8,128)(2,1)S(1)} %get-tuple-element.235), channel_id=1, source_target_pairs={{0,16},{4,20},{8,24},{12,28},{16,32},{20,36},{24,40},{28,44},{32,4... | collective-permute-start | bytes 4616 | tf_op jit(solution)/shard_map/while/body/eval_jaxpr/ppermute | solution.py:9
  219.2 14.4 %collective-permute-start.1 = (bf16[64,1536]{1,0:T(8,128)(2,1)S(1)}, bf16[64,1536]{1,0:T(8,128)(2,1)S(1)}, u32[]{:S(2)}, u32[]{:S(2)}) collective-permute-start(bf16[64,1536]{1,0:T(8,128)(2,1)S(1)} %get-tuple-element.234), channel_id=1, source_target_pairs={{0,16},{4,20},{8,24},{12,28},{16,32},{20,36},{24,40},{28,44},{32,4... | collective-permute-start | bytes 589832 | tf_op jit(solution)/shard_map/while/body/eval_jaxpr/ppermute | solution.py:9
  219.3 14.3 %collective-permute-start = (bf16[64,12]{1,0:T(8,128)(2,1)S(1)}, bf16[64,12]{1,0:T(8,128)(2,1)S(1)}, u32[]{:S(2)}, u32[]{:S(2)}) collective-permute-start(bf16[64,12]{1,0:T(8,128)(2,1)S(1)} %get-tuple-element.235), channel_id=1, source_target_pairs={{0,16},{4,20},{8,24},{12,28},{16,32},{20,36},{24,40},{28,44},{32,4... | collective-permute-start | bytes 4616 | tf_op jit(solution)/shard_map/while/body/eval_jaxpr/ppermute | solution.py:9
  235.3 12.5 %collective-permute-start.1 = (bf16[64,1536]{1,0:T(8,128)(2,1)S(1)}, bf16[64,1536]{1,0:T(8,128)(2,1)S(1)}, u32[]{:S(2)}, u32[]{:S(2)}) collective-permute-start(bf16[64,1536]{1,0:T(8,128)(2,1)S(1)} %get-tuple-element.234), channel_id=1, source_target_pairs={{0,16},{4,20},{8,24},{12,28},{16,32},{20,36},{24,40},{28,44},{32,4... | collective-permute-start | bytes 589832 | tf_op jit(solution)/shard_map/while/body/eval_jaxpr/ppermute | solution.py:9
  235.4 12.4 %collective-permute-start = (bf16[64,12]{1,0:T(8,128)(2,1)S(1)}, bf16[64,12]{1,0:T(8,128)(2,1)S(1)}, u32[]{:S(2)}, u32[]{:S(2)}) collective-permute-start(bf16[64,12]{1,0:T(8,128)(2,1)S(1)} %get-tuple-element.235), channel_id=1, source_target_pairs={{0,16},{4,20},{8,24},{12,28},{16,32},{20,36},{24,40},{28,44},{32,4... | collective-permute-start | bytes 4616 | tf_op jit(solution)/shard_map/while/body/eval_jaxpr/ppermute | solution.py:9
  249.5 11.8 %collective-permute-start.1 = (bf16[64,1536]{1,0:T(8,128)(2,1)S(1)}, bf16[64,1536]{1,0:T(8,128)(2,1)S(1)}, u32[]{:S(2)}, u32[]{:S(2)}) collective-permute-start(bf16[64,1536]{1,0:T(8,128)(2,1)S(1)} %get-tuple-element.234), channel_id=1, source_target_pairs={{0,16},{4,20},{8,24},{12,28},{16,32},{20,36},{24,40},{28,44},{32,4... | collective-permute-start | bytes 589832 | tf_op jit(solution)/shard_map/while/body/eval_jaxpr/ppermute | solution.py:9
  263.0 11.8 %collective-permute-start.1 = (bf16[64,1536]{1,0:T(8,128)(2,1)S(1)}, bf16[64,1536]{1,0:T(8,128)(2,1)S(1)}, u32[]{:S(2)}, u32[]{:S(2)}) collective-permute-start(bf16[64,1536]{1,0:T(8,128)(2,1)S(1)} %get-tuple-element.234), channel_id=1, source_target_pairs={{0,16},{4,20},{8,24},{12,28},{16,32},{20,36},{24,40},{28,44},{32,4... | collective-permute-start | bytes 589832 | tf_op jit(solution)/shard_map/while/body/eval_jaxpr/ppermute | solution.py:9
  263.0 11.7 %collective-permute-start = (bf16[64,12]{1,0:T(8,128)(2,1)S(1)}, bf16[64,12]{1,0:T(8,128)(2,1)S(1)}, u32[]{:S(2)}, u32[]{:S(2)}) collective-permute-start(bf16[64,12]{1,0:T(8,128)(2,1)S(1)} %get-tuple-element.235), channel_id=1, source_target_pairs={{0,16},{4,20},{8,24},{12,28},{16,32},{20,36},{24,40},{28,44},{32,4... | collective-permute-start | bytes 4616 | tf_op jit(solution)/shard_map/while/body/eval_jaxpr/ppermute | solution.py:9
  (6 other events, 55.7 us)
Sparse Core Ops, SparseCore 0:
  277.2 85.6 all-reduce.1
where the time goes:
time: 372 us; the launch traced here: 371 us
  waiting for transfers between devices  239 us (64%)
  starting transfers between devices  54.3 us (15%)
  local copies, waits for them, and re-layouts  23 us (6%)
  matrix products  22.6 us (6%)
  blocking collectives  17.7 us (5%)
  between operations  13.5 us (4%)
    ppermute x36, waiting for transfers between devices, passed_along(): return lax.ppermute(x, axis, [(i, (i + by) % size) for i in range(size)])  153 us
    psum x1, waiting for transfers between devices, per_device(): product = lax.psum(running, 'team')  85.8 us
    ppermute x36, starting transfers between devices, passed_along(): return lax.ppermute(x, axis, [(i, (i + by) % size) for i in range(size)])  54.3 us
    dot_general x16, matrix products, contribute(): lax.dot_general(scaled, cov_slab, (((1,), (1,)), ((), ())), preferred_ele...  22.6 us
    unnamed x5, local copies, waits for them, and re-layouts  15.1 us
    all_gather x1, blocking collectives, per_device(): lax.all_gather(loadings, 'team', axis=1, tiled=True)  10.4 us
  transfers between devices with their start and end apart: 37, of which 17 were waited for; matrix products, arithmetic and copies ran while one was open for 5% of the time, Pallas kernels for 0%

commit v1 on v0

--- a/solution.py
+++ b/solution.py
@@ -2,6 +2,7 @@
 import jax.numpy as jnp
 from jax import lax
 from jax.sharding import PartitionSpec as P
+from jax.lax import all_gather
 
 
 def passed_along(x, axis, by):
@@ -63,7 +64,7 @@
         return (contribute(partial_sum, moving, base_stop - stop_num), moving)
 
     running, _ = lax.fori_loop(1, cycle_stops, onward, (running, start_block))
-    product = lax.psum(running, "team")
+    product = jnp.sum(all_gather(running, "team"), 0)
     return product
 
 

time: 372 us -> 317 us (0.85)
  waiting for transfers between devices: 239 us -> 153 us
  blocking collectives: 17.7 us -> 63.5 us
  between operations: 13.5 us -> 0.06 us
    psum x1 -> x0, waiting for transfers between devices: 85.8 us -> none  [per_device(): product = lax.psum(running, 'team')]
    all_gather x0 -> x1, blocking collectives: none -> 45.7 us  [per_device(): product = jnp.sum(all_gather(running, 'team'), 0)]
    unnamed x5 -> x2, local copies, waits for them, and re-layouts: 15.1 us -> 13 us
  transfers between devices with their start and end apart: 37 -> 36, of which waited for: 17 -> 16; matrix products, arithmetic and copies ran while one was open for 5% -> 6% of each run, Pallas kernels for 0% -> 0%
where the time goes in v1:
time: 317 us; the launch traced here: 316 us
  waiting for transfers between devices  153 us (48%)
  blocking collectives  63.5 us (20%)
  starting transfers between devices  54.6 us (17%)
  matrix products  22.5 us (7%)
  local copies, waits for them, and re-layouts  20.9 us (7%)
    ppermute x36, waiting for transfers between devices, passed_along(): return lax.ppermute(x, axis, [(i, (i + by) % size) for i in range(size)])  153 us
    ppermute x36, starting transfers between devices, passed_along(): return lax.ppermute(x, axis, [(i, (i + by) % size) for i in range(size)])  54.6 us
    all_gather x1, blocking collectives, per_device(): product = jnp.sum(all_gather(running, 'team'), 0)  45.7 us
    dot_general x16, matrix products, contribute(): lax.dot_general(scaled, cov_slab, (((1,), (1,)), ((), ())), preferred_ele...  22.5 us
    unnamed x2, local copies, waits for them, and re-layouts  13 us
    all_gather x1, blocking collectives, per_device(): lax.all_gather(loadings, 'team', axis=1, tiled=True)  10.4 us
    all_gather x1, blocking collectives, per_device(): lax.all_gather(scales, 'team', axis=1, tiled=True)  7.35 us
  transfers between devices with their start and end apart: 36, of which 16 were waited for; matrix products, arithmetic and copies ran while one was open for 6% of the time, Pallas kernels for 0%

profile of v1, /device:TPU:1, one launch (start us, length us, event | category | flops | bytes accessed | tf_op | source)
XLA Modules:
  0.0 316.3 jit_solution(6297362508874855521)
XLA Ops:
  0.0 10.4 %all_gather.12 = bf16[64,1536]{1,0:T(8,128)(2,1)S(1)} all-gather(bf16[64,384]{1,0:T(8,128)(2,1)} %param.5), channel_id=1, replica_groups=mesh['blk'=64,'team'=4] {'team'}, dimensions={1}, use_global_device_ids=true | all-gather | bytes 245760 | tf_op jit(solution)/shard_map/all_gather | solution.py:22
  10.4 2.9 collective-permute-start.3
  13.3 7.4 %all-gather.1 = bf16[4,3,64]{2,1,0:T(4,128)(2,1)S(1)} all-gather(bf16[1,3,64]{2,1,0:T(4,128)(2,1)} %bitcast.57), channel_id=1, replica_groups=mesh['blk'=64,'team'=4] {'team'}, dimensions={0}, use_global_device_ids=true | all-gather | bytes 1920 | tf_op jit(solution)/shard_map/all_gather | solution.py:23
  20.6 2.9 collective-permute-start.5
  24.7 6.3 %collective-permute-done.5 = bf16[64,12]{0,1:T(8,128)(2,1)S(1)} collective-permute-done((bf16[64,12]{0,1:T(8,128)(2,1)S(1)}, bf16[64,12]{0,1:T(8,128)(2,1)S(1)}, u32[]{:S(2)}, u32[]{:S(2)}) %collective-permute-start.5) | collective-permute-done | bytes 1568 | tf_op jit(solution)/shard_map/ppermute | solution.py:10
  31.7 4.4 %constant_dynamic-slice_fusion = bf16[256,1,1,1536]{3,1,2,0:T(2,128)(2,1)S(1)} fusion(bf16[256,16,1,1536]{3,1,2,0:T(8,128)(2,1)} %param.7, s32[]{:T(128)S(6)} %select_n.61), kind=kLoop, calls=%fused_computation.27 | loop fusion | bytes 1572868 | tf_op jit(solution)/shard_map/jit(dynamic_index_in_dim)/dynamic_slice | solution.py:50
  36.1 13.0 %copy.27 = bf16[256,16,1,1536]{3,0,1,2:T(8,128)(2,1)} copy(bf16[256,16,1,1536]{3,1,2,0:T(8,128)(2,1)} %param.7) | data formatting | bytes 25165824 | tf_op args[2]
  50.3 219.6 %while.19 = (s32[]{:T(128)}, f32[64,256]{1,0:T(8,128)S(1)}, bf16[64,1536]{1,0:T(8,128)(2,1)S(1)}, bf16[64,12]{1,0:T(8,128)(2,1)S(1)}, s32[]{:T(128)}, /*index=5*...) while((s32[]{:T(128)}, f32[64,256]{1,0:T(8,128)S(1)}, ...), condition=%wide.region_1.2_spmd, body=%wide.region_0.1_spmd.sunk | while | flops 50642960 | bytes 3091284 | solution.py:66
  50.3 2.6 collective-permute-start.1
  52.9 3.8 %collective-permute-start = (bf16[64,12]{1,0:T(8,128)(2,1)S(1)}, bf16[64,12]{1,0:T(8,128)(2,1)S(1)}, u32[]{:S(2)}, u32[]{:S(2)}) collective-permute-start(bf16[64,12]{1,0:T(8,128)(2,1)S(1)} %get-tuple-element.235), channel_id=1, source_target_pairs={{0,16},{4,20},{8,24},{12,28},{16,32},{20,36},{24,40},{28,44},{32,4... | collective-permute-start | bytes 4616 | tf_op jit(solution)/shard_map/while/body/eval_jaxpr/ppermute | solution.py:10
  56.7 8.5 %collective-permute-done = bf16[64,12]{1,0:T(8,128)(2,1)S(1)} collective-permute-done((bf16[64,12]{1,0:T(8,128)(2,1)S(1)}, bf16[64,12]{1,0:T(8,128)(2,1)S(1)}, u32[]{:S(2)}, u32[]{:S(2)}) %collective-permute-start) | collective-permute-done | bytes 1568 | tf_op jit(solution)/shard_map/while/body/eval_jaxpr/ppermute | solution.py:10
  67.6 5.7 %collective-permute-start = (bf16[64,12]{1,0:T(8,128)(2,1)S(1)}, bf16[64,12]{1,0:T(8,128)(2,1)S(1)}, u32[]{:S(2)}, u32[]{:S(2)}) collective-permute-start(bf16[64,12]{1,0:T(8,128)(2,1)S(1)} %get-tuple-element.235), channel_id=1, source_target_pairs={{0,16},{4,20},{8,24},{12,28},{16,32},{20,36},{24,40},{28,44},{32,4... | collective-permute-start | bytes 4616 | tf_op jit(solution)/shard_map/while/body/eval_jaxpr/ppermute | solution.py:10
  73.3 11.1 %collective-permute-done = bf16[64,12]{1,0:T(8,128)(2,1)S(1)} collective-permute-done((bf16[64,12]{1,0:T(8,128)(2,1)S(1)}, bf16[64,12]{1,0:T(8,128)(2,1)S(1)}, u32[]{:S(2)}, u32[]{:S(2)}) %collective-permute-start) | collective-permute-done | bytes 1568 | tf_op jit(solution)/shard_map/while/body/eval_jaxpr/ppermute | solution.py:10
  88.3 10.4 %collective-permute-done = bf16[64,12]{1,0:T(8,128)(2,1)S(1)} collective-permute-done((bf16[64,12]{1,0:T(8,128)(2,1)S(1)}, bf16[64,12]{1,0:T(8,128)(2,1)S(1)}, u32[]{:S(2)}, u32[]{:S(2)}) %collective-permute-start) | collective-permute-done | bytes 1568 | tf_op jit(solution)/shard_map/while/body/eval_jaxpr/ppermute | solution.py:10
  100.5 3.6 %collective-permute-start = (bf16[64,12]{1,0:T(8,128)(2,1)S(1)}, bf16[64,12]{1,0:T(8,128)(2,1)S(1)}, u32[]{:S(2)}, u32[]{:S(2)}) collective-permute-start(bf16[64,12]{1,0:T(8,128)(2,1)S(1)} %get-tuple-element.235), channel_id=1, source_target_pairs={{0,16},{4,20},{8,24},{12,28},{16,32},{20,36},{24,40},{28,44},{32,4... | collective-permute-start | bytes 4616 | tf_op jit(solution)/shard_map/while/body/eval_jaxpr/ppermute | solution.py:10
  104.1 8.2 %collective-permute-done = bf16[64,12]{1,0:T(8,128)(2,1)S(1)} collective-permute-done((bf16[64,12]{1,0:T(8,128)(2,1)S(1)}, bf16[64,12]{1,0:T(8,128)(2,1)S(1)}, u32[]{:S(2)}, u32[]{:S(2)}) %collective-permute-start) | collective-permute-done | bytes 1568 | tf_op jit(solution)/shard_map/while/body/eval_jaxpr/ppermute | solution.py:10
  114.1 4.6 %collective-permute-start = (bf16[64,12]{1,0:T(8,128)(2,1)S(1)}, bf16[64,12]{1,0:T(8,128)(2,1)S(1)}, u32[]{:S(2)}, u32[]{:S(2)}) collective-permute-start(bf16[64,12]{1,0:T(8,128)(2,1)S(1)} %get-tuple-element.235), channel_id=1, source_target_pairs={{0,16},{4,20},{8,24},{12,28},{16,32},{20,36},{24,40},{28,44},{32,4... | collective-permute-start | bytes 4616 | tf_op jit(solution)/shard_map/while/body/eval_jaxpr/ppermute | solution.py:10
  118.7 7.1 %collective-permute-done = bf16[64,12]{1,0:T(8,128)(2,1)S(1)} collective-permute-done((bf16[64,12]{1,0:T(8,128)(2,1)S(1)}, bf16[64,12]{1,0:T(8,128)(2,1)S(1)}, u32[]{:S(2)}, u32[]{:S(2)}) %collective-permute-start) | collective-permute-done | bytes 1568 | tf_op jit(solution)/shard_map/while/body/eval_jaxpr/ppermute | solution.py:10
  127.6 5.4 %collective-permute-start = (bf16[64,12]{1,0:T(8,128)(2,1)S(1)}, bf16[64,12]{1,0:T(8,128)(2,1)S(1)}, u32[]{:S(2)}, u32[]{:S(2)}) collective-permute-start(bf16[64,12]{1,0:T(8,128)(2,1)S(1)} %get-tuple-element.235), channel_id=1, source_target_pairs={{0,16},{4,20},{8,24},{12,28},{16,32},{20,36},{24,40},{28,44},{32,4... | collective-permute-start | bytes 4616 | tf_op jit(solution)/shard_map/while/body/eval_jaxpr/ppermute | solution.py:10
  132.9 6.3 %collective-permute-done = bf16[64,12]{1,0:T(8,128)(2,1)S(1)} collective-permute-done((bf16[64,12]{1,0:T(8,128)(2,1)S(1)}, bf16[64,12]{1,0:T(8,128)(2,1)S(1)}, u32[]{:S(2)}, u32[]{:S(2)}) %collective-permute-start) | collective-permute-done | bytes 1568 | tf_op jit(solution)/shard_map/while/body/eval_jaxpr/ppermute | solution.py:10
  141.2 6.4 %collective-permute-start = (bf16[64,12]{1,0:T(8,128)(2,1)S(1)}, bf16[64,12]{1,0:T(8,128)(2,1)S(1)}, u32[]{:S(2)}, u32[]{:S(2)}) collective-permute-start(bf16[64,12]{1,0:T(8,128)(2,1)S(1)} %get-tuple-element.235), channel_id=1, source_target_pairs={{0,16},{4,20},{8,24},{12,28},{16,32},{20,36},{24,40},{28,44},{32,4... | collective-permute-start | bytes 4616 | tf_op jit(solution)/shard_map/while/body/eval_jaxpr/ppermute | solution.py:10
  147.6 5.0 %collective-permute-done = bf16[64,12]{1,0:T(8,128)(2,1)S(1)} collective-permute-done((bf16[64,12]{1,0:T(8,128)(2,1)S(1)}, bf16[64,12]{1,0:T(8,128)(2,1)S(1)}, u32[]{:S(2)}, u32[]{:S(2)}) %collective-permute-start) | collective-permute-done | bytes 1568 | tf_op jit(solution)/shard_map/while/body/eval_jaxpr/ppermute | solution.py:10
  156.0 3.0 collective-permute-start
  159.0 7.0 %collective-permute-done = bf16[64,12]{1,0:T(8,128)(2,1)S(1)} collective-permute-done((bf16[64,12]{1,0:T(8,128)(2,1)S(1)}, bf16[64,12]{1,0:T(8,128)(2,1)S(1)}, u32[]{:S(2)}, u32[]{:S(2)}) %collective-permute-start) | collective-permute-done | bytes 1568 | tf_op jit(solution)/shard_map/while/body/eval_jaxpr/ppermute | solution.py:10
  170.4 10.0 %collective-permute-done = bf16[64,12]{1,0:T(8,128)(2,1)S(1)} collective-permute-done((bf16[64,12]{1,0:T(8,128)(2,1)S(1)}, bf16[64,12]{1,0:T(8,128)(2,1)S(1)}, u32[]{:S(2)}, u32[]{:S(2)}) %collective-permute-start) | collective-permute-done | bytes 1568 | tf_op jit(solution)/shard_map/while/body/eval_jaxpr/ppermute | solution.py:10
  183.6 12.2 %collective-permute-done = bf16[64,12]{1,0:T(8,128)(2,1)S(1)} collective-permute-done((bf16[64,12]{1,0:T(8,128)(2,1)S(1)}, bf16[64,12]{1,0:T(8,128)(2,1)S(1)}, u32[]{:S(2)}, u32[]{:S(2)}) %collective-permute-start) | collective-permute-done | bytes 1568 | tf_op jit(solution)/shard_map/while/body/eval_jaxpr/ppermute | solution.py:10
  197.7 13.2 %collective-permute-done = bf16[64,12]{1,0:T(8,128)(2,1)S(1)} collective-permute-done((bf16[64,12]{1,0:T(8,128)(2,1)S(1)}, bf16[64,12]{1,0:T(8,128)(2,1)S(1)}, u32[]{:S(2)}, u32[]{:S(2)}) %collective-permute-start) | collective-permute-done | bytes 1568 | tf_op jit(solution)/shard_map/while/body/eval_jaxpr/ppermute | solution.py:10
  212.9 14.1 %collective-permute-done = bf16[64,12]{1,0:T(8,128)(2,1)S(1)} collective-permute-done((bf16[64,12]{1,0:T(8,128)(2,1)S(1)}, bf16[64,12]{1,0:T(8,128)(2,1)S(1)}, u32[]{:S(2)}, u32[]{:S(2)}) %collective-permute-start) | collective-permute-done | bytes 1568 | tf_op jit(solution)/shard_map/while/body/eval_jaxpr/ppermute | solution.py:10
  228.9 12.3 %collective-permute-done = bf16[64,12]{1,0:T(8,128)(2,1)S(1)} collective-permute-done((bf16[64,12]{1,0:T(8,128)(2,1)S(1)}, bf16[64,12]{1,0:T(8,128)(2,1)S(1)}, u32[]{:S(2)}, u32[]{:S(2)}) %collective-permute-start) | collective-permute-done | bytes 1568 | tf_op jit(solution)/shard_map/while/body/eval_jaxpr/ppermute | solution.py:10
  243.7 11.0 %collective-permute-done = bf16[64,12]{1,0:T(8,128)(2,1)S(1)} collective-permute-done((bf16[64,12]{1,0:T(8,128)(2,1)S(1)}, bf16[64,12]{1,0:T(8,128)(2,1)S(1)}, u32[]{:S(2)}, u32[]{:S(2)}) %collective-permute-start) | collective-permute-done | bytes 1568 | tf_op jit(solution)/shard_map/while/body/eval_jaxpr/ppermute | solution.py:10
  257.9 10.3 %collective-permute-done = bf16[64,12]{1,0:T(8,128)(2,1)S(1)} collective-permute-done((bf16[64,12]{1,0:T(8,128)(2,1)S(1)}, bf16[64,12]{1,0:T(8,128)(2,1)S(1)}, u32[]{:S(2)}, u32[]{:S(2)}) %collective-permute-start) | collective-permute-done | bytes 1568 | tf_op jit(solution)/shard_map/while/body/eval_jaxpr/ppermute | solution.py:10
  269.9 45.7 %all-gather = f32[256,256]{1,0:T(8,128)S(1)} all-gather(f32[64,256]{1,0:T(8,128)S(1)} %get-tuple-element.160), channel_id=2, replica_groups=mesh['blk'=64,'team'=4] {'team'}, dimensions={0}, use_global_device_ids=true | all-gather | bytes 327680 | tf_op jit(solution)/shard_map/all_gather | solution.py:67
  (115 shorter events, 40.8 us)
Async XLA Ops:
  10.4 20.6 %collective-permute-start.2 = (bf16[64,1536]{1,0:T(8,128)(2,1)S(1)}, bf16[64,1536]{1,0:T(8,128)(2,1)S(1)}, u32[]{:S(2)}, u32[]{:S(2)}) collective-permute-start(bf16[64,1536]{1,0:T(8,128)(2,1)S(1)} %all_gather.12), channel_id=1, source_target_pairs={{0,4},{4,8},{8,12},{12,16},{16,20},{20,24},{24,28},{28,32},{32,36}... | collective-permute-start | bytes 589832 | tf_op jit(solution)/shard_map/ppermute | solution.py:10
  10.4 39.0 %collective-permute-start.3 = (bf16[64,1536]{1,0:T(8,128)(2,1)S(1)}, bf16[64,1536]{1,0:T(8,128)(2,1)S(1)}, u32[]{:S(2)}, u32[]{:S(2)}) collective-permute-start(bf16[64,1536]{1,0:T(8,128)(2,1)S(1)} %all_gather.12), channel_id=1, source_target_pairs={{0,8},{4,12},{8,16},{12,20},{16,24},{20,28},{24,32},{28,36},{32,40... | collective-permute-start | bytes 589832 | tf_op jit(solution)/shard_map/ppermute | solution.py:10
  23.5 25.6 %collective-permute-start.6 = (bf16[64,12]{0,1:T(8,128)(2,1)S(1)}, bf16[64,12]{0,1:T(8,128)(2,1)S(1)}, u32[]{:S(2)}, u32[]{:S(2)}) collective-permute-start(bf16[64,12]{0,1:T(8,128)(2,1)S(1)} %bitcast.52), channel_id=1, source_target_pairs={{0,8},{4,12},{8,16},{12,20},{16,24},{20,28},{24,32},{28,36},{32,40... | collective-permute-start | bytes 4616 | tf_op jit(solution)/shard_map/ppermute | solution.py:10
  31.0 18.1 %collective-permute-start.7 = (bf16[64,12]{0,1:T(8,128)(2,1)S(1)}, bf16[64,12]{0,1:T(8,128)(2,1)S(1)}, u32[]{:S(2)}, u32[]{:S(2)}) collective-permute-start(bf16[64,12]{0,1:T(8,128)(2,1)S(1)} %collective-permute-done.5), channel_id=1, source_target_pairs={{0,8},{4,12},{8,16},{12,20},{16,24},{20,28},{24,32},{28,36},{32,40... | collective-permute-start | bytes 4616 | tf_op jit(solution)/shard_map/ppermute | solution.py:10
  31.0 18.4 %collective-permute-start.4 = (bf16[64,1536]{1,0:T(8,128)(2,1)S(1)}, bf16[64,1536]{1,0:T(8,128)(2,1)S(1)}, u32[]{:S(2)}, u32[]{:S(2)}) collective-permute-start(bf16[64,1536]{1,0:T(8,128)(2,1)S(1)} %collective-permute-done.2), channel_id=1, source_target_pairs={{0,8},{4,12},{8,16},{12,20},{16,24},{20,28},{24,32},{28,36},{32,40... | collective-permute-start | bytes 589832 | tf_op jit(solution)/shard_map/ppermute | solution.py:10
  50.3 14.9 %collective-permute-start.1 = (bf16[64,1536]{1,0:T(8,128)(2,1)S(1)}, bf16[64,1536]{1,0:T(8,128)(2,1)S(1)}, u32[]{:S(2)}, u32[]{:S(2)}) collective-permute-start(bf16[64,1536]{1,0:T(8,128)(2,1)S(1)} %get-tuple-element.234), channel_id=1, source_target_pairs={{0,16},{4,20},{8,24},{12,28},{16,32},{20,36},{24,40},{28,44},{32,4... | collective-permute-start | bytes 589832 | tf_op jit(solution)/shard_map/while/body/eval_jaxpr/ppermute | solution.py:10
  52.9 12.3 %collective-permute-start = (bf16[64,12]{1,0:T(8,128)(2,1)S(1)}, bf16[64,12]{1,0:T(8,128)(2,1)S(1)}, u32[]{:S(2)}, u32[]{:S(2)}) collective-permute-start(bf16[64,12]{1,0:T(8,128)(2,1)S(1)} %get-tuple-element.235), channel_id=1, source_target_pairs={{0,16},{4,20},{8,24},{12,28},{16,32},{20,36},{24,40},{28,44},{32,4... | collective-permute-start | bytes 4616 | tf_op jit(solution)/shard_map/while/body/eval_jaxpr/ppermute | solution.py:10
  66.9 17.6 %collective-permute-start.1 = (bf16[64,1536]{1,0:T(8,128)(2,1)S(1)}, bf16[64,1536]{1,0:T(8,128)(2,1)S(1)}, u32[]{:S(2)}, u32[]{:S(2)}) collective-permute-start(bf16[64,1536]{1,0:T(8,128)(2,1)S(1)} %get-tuple-element.234), channel_id=1, source_target_pairs={{0,16},{4,20},{8,24},{12,28},{16,32},{20,36},{24,40},{28,44},{32,4... | collective-permute-start | bytes 589832 | tf_op jit(solution)/shard_map/while/body/eval_jaxpr/ppermute | solution.py:10
  67.6 16.8 %collective-permute-start = (bf16[64,12]{1,0:T(8,128)(2,1)S(1)}, bf16[64,12]{1,0:T(8,128)(2,1)S(1)}, u32[]{:S(2)}, u32[]{:S(2)}) collective-permute-start(bf16[64,12]{1,0:T(8,128)(2,1)S(1)} %get-tuple-element.235), channel_id=1, source_target_pairs={{0,16},{4,20},{8,24},{12,28},{16,32},{20,36},{24,40},{28,44},{32,4... | collective-permute-start | bytes 4616 | tf_op jit(solution)/shard_map/while/body/eval_jaxpr/ppermute | solution.py:10
  86.2 12.5 %collective-permute-start.1 = (bf16[64,1536]{1,0:T(8,128)(2,1)S(1)}, bf16[64,1536]{1,0:T(8,128)(2,1)S(1)}, u32[]{:S(2)}, u32[]{:S(2)}) collective-permute-start(bf16[64,1536]{1,0:T(8,128)(2,1)S(1)} %get-tuple-element.234), channel_id=1, source_target_pairs={{0,16},{4,20},{8,24},{12,28},{16,32},{20,36},{24,40},{28,44},{32,4... | collective-permute-start | bytes 589832 | tf_op jit(solution)/shard_map/while/body/eval_jaxpr/ppermute | solution.py:10
  86.3 12.4 %collective-permute-start = (bf16[64,12]{1,0:T(8,128)(2,1)S(1)}, bf16[64,12]{1,0:T(8,128)(2,1)S(1)}, u32[]{:S(2)}, u32[]{:S(2)}) collective-permute-start(bf16[64,12]{1,0:T(8,128)(2,1)S(1)} %get-tuple-element.235), channel_id=1, source_target_pairs={{0,16},{4,20},{8,24},{12,28},{16,32},{20,36},{24,40},{28,44},{32,4... | collective-permute-start | bytes 4616 | tf_op jit(solution)/shard_map/while/body/eval_jaxpr/ppermute | solution.py:10
  100.4 11.9 %collective-permute-start.1 = (bf16[64,1536]{1,0:T(8,128)(2,1)S(1)}, bf16[64,1536]{1,0:T(8,128)(2,1)S(1)}, u32[]{:S(2)}, u32[]{:S(2)}) collective-permute-start(bf16[64,1536]{1,0:T(8,128)(2,1)S(1)} %get-tuple-element.234), channel_id=1, source_target_pairs={{0,16},{4,20},{8,24},{12,28},{16,32},{20,36},{24,40},{28,44},{32,4... | collective-permute-start | bytes 589832 | tf_op jit(solution)/shard_map/while/body/eval_jaxpr/ppermute | solution.py:10
  100.5 11.8 %collective-permute-start = (bf16[64,12]{1,0:T(8,128)(2,1)S(1)}, bf16[64,12]{1,0:T(8,128)(2,1)S(1)}, u32[]{:S(2)}, u32[]{:S(2)}) collective-permute-start(bf16[64,12]{1,0:T(8,128)(2,1)S(1)} %get-tuple-element.235), channel_id=1, source_target_pairs={{0,16},{4,20},{8,24},{12,28},{16,32},{20,36},{24,40},{28,44},{32,4... | collective-permute-start | bytes 4616 | tf_op jit(solution)/shard_map/while/body/eval_jaxpr/ppermute | solution.py:10
  114.0 11.8 %collective-permute-start.1 = (bf16[64,1536]{1,0:T(8,128)(2,1)S(1)}, bf16[64,1536]{1,0:T(8,128)(2,1)S(1)}, u32[]{:S(2)}, u32[]{:S(2)}) collective-permute-start(bf16[64,1536]{1,0:T(8,128)(2,1)S(1)} %get-tuple-element.234), channel_id=1, source_target_pairs={{0,16},{4,20},{8,24},{12,28},{16,32},{20,36},{24,40},{28,44},{32,4... | collective-permute-start | bytes 589832 | tf_op jit(solution)/shard_map/while/body/eval_jaxpr/ppermute | solution.py:10
  114.1 11.7 %collective-permute-start = (bf16[64,12]{1,0:T(8,128)(2,1)S(1)}, bf16[64,12]{1,0:T(8,128)(2,1)S(1)}, u32[]{:S(2)}, u32[]{:S(2)}) collective-permute-start(bf16[64,12]{1,0:T(8,128)(2,1)S(1)} %get-tuple-element.235), channel_id=1, source_target_pairs={{0,16},{4,20},{8,24},{12,28},{16,32},{20,36},{24,40},{28,44},{32,4... | collective-permute-start | bytes 4616 | tf_op jit(solution)/shard_map/while/body/eval_jaxpr/ppermute | solution.py:10
  127.5 11.7 %collective-permute-start.1 = (bf16[64,1536]{1,0:T(8,128)(2,1)S(1)}, bf16[64,1536]{1,0:T(8,128)(2,1)S(1)}, u32[]{:S(2)}, u32[]{:S(2)}) collective-permute-start(bf16[64,1536]{1,0:T(8,128)(2,1)S(1)} %get-tuple-element.234), channel_id=1, source_target_pairs={{0,16},{4,20},{8,24},{12,28},{16,32},{20,36},{24,40},{28,44},{32,4... | collective-permute-start | bytes 589832 | tf_op jit(solution)/shard_map/while/body/eval_jaxpr/ppermute | solution.py:10
  141.0 11.7 %collective-permute-start.1 = (bf16[64,1536]{1,0:T(8,128)(2,1)S(1)}, bf16[64,1536]{1,0:T(8,128)(2,1)S(1)}, u32[]{:S(2)}, u32[]{:S(2)}) collective-permute-start(bf16[64,1536]{1,0:T(8,128)(2,1)S(1)} %get-tuple-element.234), channel_id=1, source_target_pairs={{0,16},{4,20},{8,24},{12,28},{16,32},{20,36},{24,40},{28,44},{32,4... | collective-permute-start | bytes 589832 | tf_op jit(solution)/shard_map/while/body/eval_jaxpr/ppermute | solution.py:10
  154.4 11.7 %collective-permute-start.1 = (bf16[64,1536]{1,0:T(8,128)(2,1)S(1)}, bf16[64,1536]{1,0:T(8,128)(2,1)S(1)}, u32[]{:S(2)}, u32[]{:S(2)}) collective-permute-start(bf16[64,1536]{1,0:T(8,128)(2,1)S(1)} %get-tuple-element.234), channel_id=1, source_target_pairs={{0,16},{4,20},{8,24},{12,28},{16,32},{20,36},{24,40},{28,44},{32,4... | collective-permute-start | bytes 589832 | tf_op jit(solution)/shard_map/while/body/eval_jaxpr/ppermute | solution.py:10
  167.8 12.6 %collective-permute-start.1 = (bf16[64,1536]{1,0:T(8,128)(2,1)S(1)}, bf16[64,1536]{1,0:T(8,128)(2,1)S(1)}, u32[]{:S(2)}, u32[]{:S(2)}) collective-permute-start(bf16[64,1536]{1,0:T(8,128)(2,1)S(1)} %get-tuple-element.234), channel_id=1, source_target_pairs={{0,16},{4,20},{8,24},{12,28},{16,32},{20,36},{24,40},{28,44},{32,4... | collective-permute-start | bytes 589832 | tf_op jit(solution)/shard_map/while/body/eval_jaxpr/ppermute | solution.py:10
  168.5 11.8 %collective-permute-start = (bf16[64,12]{1,0:T(8,128)(2,1)S(1)}, bf16[64,12]{1,0:T(8,128)(2,1)S(1)}, u32[]{:S(2)}, u32[]{:S(2)}) collective-permute-start(bf16[64,12]{1,0:T(8,128)(2,1)S(1)} %get-tuple-element.235), channel_id=1, source_target_pairs={{0,16},{4,20},{8,24},{12,28},{16,32},{20,36},{24,40},{28,44},{32,4... | collective-permute-start | bytes 4616 | tf_op jit(solution)/shard_map/while/body/eval_jaxpr/ppermute | solution.py:10
  182.1 13.7 %collective-permute-start.1 = (bf16[64,1536]{1,0:T(8,128)(2,1)S(1)}, bf16[64,1536]{1,0:T(8,128)(2,1)S(1)}, u32[]{:S(2)}, u32[]{:S(2)}) collective-permute-start(bf16[64,1536]{1,0:T(8,128)(2,1)S(1)} %get-tuple-element.234), channel_id=1, source_target_pairs={{0,16},{4,20},{8,24},{12,28},{16,32},{20,36},{24,40},{28,44},{32,4... | collective-permute-start | bytes 589832 | tf_op jit(solution)/shard_map/while/body/eval_jaxpr/ppermute | solution.py:10
  182.2 13.6 %collective-permute-start = (bf16[64,12]{1,0:T(8,128)(2,1)S(1)}, bf16[64,12]{1,0:T(8,128)(2,1)S(1)}, u32[]{:S(2)}, u32[]{:S(2)}) collective-permute-start(bf16[64,12]{1,0:T(8,128)(2,1)S(1)} %get-tuple-element.235), channel_id=1, source_target_pairs={{0,16},{4,20},{8,24},{12,28},{16,32},{20,36},{24,40},{28,44},{32,4... | collective-permute-start | bytes 4616 | tf_op jit(solution)/shard_map/while/body/eval_jaxpr/ppermute | solution.py:10
  197.5 13.4 %collective-permute-start.1 = (bf16[64,1536]{1,0:T(8,128)(2,1)S(1)}, bf16[64,1536]{1,0:T(8,128)(2,1)S(1)}, u32[]{:S(2)}, u32[]{:S(2)}) collective-permute-start(bf16[64,1536]{1,0:T(8,128)(2,1)S(1)} %get-tuple-element.234), channel_id=1, source_target_pairs={{0,16},{4,20},{8,24},{12,28},{16,32},{20,36},{24,40},{28,44},{32,4... | collective-permute-start | bytes 589832 | tf_op jit(solution)/shard_map/while/body/eval_jaxpr/ppermute | solution.py:10
  197.6 13.3 %collective-permute-start = (bf16[64,12]{1,0:T(8,128)(2,1)S(1)}, bf16[64,12]{1,0:T(8,128)(2,1)S(1)}, u32[]{:S(2)}, u32[]{:S(2)}) collective-permute-start(bf16[64,12]{1,0:T(8,128)(2,1)S(1)} %get-tuple-element.235), channel_id=1, source_target_pairs={{0,16},{4,20},{8,24},{12,28},{16,32},{20,36},{24,40},{28,44},{32,4... | collective-permute-start | bytes 4616 | tf_op jit(solution)/shard_map/while/body/eval_jaxpr/ppermute | solution.py:10
  212.7 14.3 %collective-permute-start.1 = (bf16[64,1536]{1,0:T(8,128)(2,1)S(1)}, bf16[64,1536]{1,0:T(8,128)(2,1)S(1)}, u32[]{:S(2)}, u32[]{:S(2)}) collective-permute-start(bf16[64,1536]{1,0:T(8,128)(2,1)S(1)} %get-tuple-element.234), channel_id=1, source_target_pairs={{0,16},{4,20},{8,24},{12,28},{16,32},{20,36},{24,40},{28,44},{32,4... | collective-permute-start | bytes 589832 | tf_op jit(solution)/shard_map/while/body/eval_jaxpr/ppermute | solution.py:10
  212.8 14.2 %collective-permute-start = (bf16[64,12]{1,0:T(8,128)(2,1)S(1)}, bf16[64,12]{1,0:T(8,128)(2,1)S(1)}, u32[]{:S(2)}, u32[]{:S(2)}) collective-permute-start(bf16[64,12]{1,0:T(8,128)(2,1)S(1)} %get-tuple-element.235), channel_id=1, source_target_pairs={{0,16},{4,20},{8,24},{12,28},{16,32},{20,36},{24,40},{28,44},{32,4... | collective-permute-start | bytes 4616 | tf_op jit(solution)/shard_map/while/body/eval_jaxpr/ppermute | solution.py:10
  228.7 12.5 %collective-permute-start.1 = (bf16[64,1536]{1,0:T(8,128)(2,1)S(1)}, bf16[64,1536]{1,0:T(8,128)(2,1)S(1)}, u32[]{:S(2)}, u32[]{:S(2)}) collective-permute-start(bf16[64,1536]{1,0:T(8,128)(2,1)S(1)} %get-tuple-element.234), channel_id=1, source_target_pairs={{0,16},{4,20},{8,24},{12,28},{16,32},{20,36},{24,40},{28,44},{32,4... | collective-permute-start | bytes 589832 | tf_op jit(solution)/shard_map/while/body/eval_jaxpr/ppermute | solution.py:10
  228.8 12.4 %collective-permute-start = (bf16[64,12]{1,0:T(8,128)(2,1)S(1)}, bf16[64,12]{1,0:T(8,128)(2,1)S(1)}, u32[]{:S(2)}, u32[]{:S(2)}) collective-permute-start(bf16[64,12]{1,0:T(8,128)(2,1)S(1)} %get-tuple-element.235), channel_id=1, source_target_pairs={{0,16},{4,20},{8,24},{12,28},{16,32},{20,36},{24,40},{28,44},{32,4... | collective-permute-start | bytes 4616 | tf_op jit(solution)/shard_map/while/body/eval_jaxpr/ppermute | solution.py:10
  242.9 11.8 %collective-permute-start.1 = (bf16[64,1536]{1,0:T(8,128)(2,1)S(1)}, bf16[64,1536]{1,0:T(8,128)(2,1)S(1)}, u32[]{:S(2)}, u32[]{:S(2)}) collective-permute-start(bf16[64,1536]{1,0:T(8,128)(2,1)S(1)} %get-tuple-element.234), channel_id=1, source_target_pairs={{0,16},{4,20},{8,24},{12,28},{16,32},{20,36},{24,40},{28,44},{32,4... | collective-permute-start | bytes 589832 | tf_op jit(solution)/shard_map/while/body/eval_jaxpr/ppermute | solution.py:10
  243.0 11.7 %collective-permute-start = (bf16[64,12]{1,0:T(8,128)(2,1)S(1)}, bf16[64,12]{1,0:T(8,128)(2,1)S(1)}, u32[]{:S(2)}, u32[]{:S(2)}) collective-permute-start(bf16[64,12]{1,0:T(8,128)(2,1)S(1)} %get-tuple-element.235), channel_id=1, source_target_pairs={{0,16},{4,20},{8,24},{12,28},{16,32},{20,36},{24,40},{28,44},{32,4... | collective-permute-start | bytes 4616 | tf_op jit(solution)/shard_map/while/body/eval_jaxpr/ppermute | solution.py:10
  256.4 11.8 %collective-permute-start.1 = (bf16[64,1536]{1,0:T(8,128)(2,1)S(1)}, bf16[64,1536]{1,0:T(8,128)(2,1)S(1)}, u32[]{:S(2)}, u32[]{:S(2)}) collective-permute-start(bf16[64,1536]{1,0:T(8,128)(2,1)S(1)} %get-tuple-element.234), channel_id=1, source_target_pairs={{0,16},{4,20},{8,24},{12,28},{16,32},{20,36},{24,40},{28,44},{32,4... | collective-permute-start | bytes 589832 | tf_op jit(solution)/shard_map/while/body/eval_jaxpr/ppermute | solution.py:10
  256.5 11.7 %collective-permute-start = (bf16[64,12]{1,0:T(8,128)(2,1)S(1)}, bf16[64,12]{1,0:T(8,128)(2,1)S(1)}, u32[]{:S(2)}, u32[]{:S(2)}) collective-permute-start(bf16[64,12]{1,0:T(8,128)(2,1)S(1)} %get-tuple-element.235), channel_id=1, source_target_pairs={{0,16},{4,20},{8,24},{12,28},{16,32},{20,36},{24,40},{28,44},{32,4... | collective-permute-start | bytes 4616 | tf_op jit(solution)/shard_map/while/body/eval_jaxpr/ppermute | solution.py:10
  (4 other events, 43.5 us)
